TPU v7x, 512 devices: a whole 4x4x16 slice. The times are simulated.
512 devices in a mesh: req: 128 (over z, y, core), tp: 4 (over x).
Axes of the slice: x: 4, y: 4, z: 16, core: 2. Of those that a mesh axis runs over, the one named last changes fastest.
Arguments:
- states: bfloat16 [32768, 3072], P('req', 'tp'), may hold values from -12 to 12
- query_weight: bfloat16 [3072, 1536], P(None, 'tp'), may hold values from -0.75 to 0.75
- key_value_weight: bfloat16 [3072, 512], P(None, 'tp'), may hold values from -0.75 to 0.75
- lengths: int32 [128], P('req'), may hold values from 1 to 256, 16384 in all
- adapter_ids: int32 [128], P('req'), may hold values from 0 to 63, as said below
- adapter_slot: int32 [64], replicated, may hold values from 0 to 127, as said below
- down_store: bfloat16 [128, 3072, 32], P('req', 'tp'), may hold values from -0.109375 to 0.109375
- query_up_store: bfloat16 [128, 16, 1536], P('req', None, 'tp'), may hold values from -1.5 to 1.5
- key_value_store: bfloat16 [128, 16, 512], P('req', None, 'tp'), may hold values from -1.5 to 1.5
Outputs:
- context: bfloat16 [32768, 1536], P('req', 'tp')
Inputs may be any that keep to these rules, and one draw needn't show every extreme that they name: `adapter_ids`: exactly 16 distinct adapters are named among all 128 requests. `adapter_slot`: distinct adapters have distinct rows.
All inputs are finite; a program needn't handle non-finite values. No bound on the sum of `lengths` on one device may be relied on, other than what follows from the above.
Results may differ from a plain program's by a relative error of at most 0.0072.
Values may be sent and summed in bfloat16 or wider, within the bound.
No kernel may reach another device: no remote copies, remote signals or barrier semaphores. Data moves between devices by JAX's collectives and lax.ppermute only.
A program may use at most 64 MiB of HBM per device.

v0:
```python
import math
import jax
import jax.numpy as jnp
from jax import lax
from jax.sharding import PartitionSpec as P

HEADS = 12
HEAD_DIM = 128
adapter_scale = 0.5
rope_base = 100000000000.0


def rotate(field):
    half = field.shape[-1] // 2
    count = field.shape[-3]
    position = jnp.arange(count).astype(jnp.float32)
    inverse = rope_base ** (-(jnp.arange(half).astype(jnp.float32) * 2.0) / field.shape[-1])
    angle = position[:, None] * inverse[None, :]
    cosine = jnp.cos(angle)[:, None, :]
    sine = jnp.sin(angle)[:, None, :]
    first_half = field[..., :half]
    second_half = field[..., half:]
    return jnp.concatenate(
        [first_half * cosine - second_half * sine, second_half * cosine + first_half * sine],
        axis=-1,
    )


def lookup_slots(wanted, adapter_slot):
    table = jnp.arange(adapter_slot.shape[0], dtype=jnp.int32)
    matches = wanted[:, None] == table[None, :]
    return jnp.sum(jnp.where(matches, adapter_slot[None, :], 0), axis=1)


def local(
    states,
    query_weight,
    key_value_weight,
    lengths,
    adapter_ids,
    adapter_slot,
    down_store,
    query_up_store,
    key_value_store,
):
    tp_index = lax.axis_index("tp")
    req_dev = lengths.shape[0]
    rows_total = states.shape[0]
    slot_len = rows_total // req_dev
    q_cols = query_weight.shape[1]
    kv_cols = key_value_weight.shape[1]
    heads_here = q_cols // HEAD_DIM
    pooled = (
        lax.all_gather(down_store, "req", axis=0, tiled=True),
        lax.all_gather(query_up_store, "req", axis=0, tiled=True),
        lax.all_gather(key_value_store, "req", axis=0, tiled=True),
    )
    own_slots = lookup_slots(adapter_ids, adapter_slot)
    adapter_down, adapter_query, adapter_pair = (
        jnp.take(member, own_slots, axis=0) for member in pooled
    )
    full_down = lax.all_gather(adapter_down, "tp", axis=1, tiled=True)
    piece = lax.all_gather(states, "tp", axis=1, tiled=True)
    width = piece.shape[1]
    grouped = piece.reshape(req_dev, slot_len, width)
    query_total = jnp.dot(piece, query_weight, preferred_element_type=jnp.float32)
    key_value_sum = jnp.dot(piece, key_value_weight, preferred_element_type=jnp.float32)
    rank_sum = jnp.einsum("rsd,rdk->rsk", grouped, full_down, preferred_element_type=jnp.float32)
    rank_mid = rank_sum.astype(jnp.bfloat16)
    rank_cols = rank_mid.shape[2] // 2
    query_addition = jnp.einsum(
        "rsk,rkc->rsc",
        rank_mid[:, :, :rank_cols],
        adapter_query,
        preferred_element_type=jnp.float32,
    ).reshape(rows_total, q_cols)
    key_value_extra = jnp.einsum(
        "rsk,rkc->rsc", rank_mid[:, :, rank_cols:], adapter_pair, preferred_element_type=jnp.float32
    ).reshape(rows_total, kv_cols)
    query_plain = query_total + adapter_scale * query_addition
    key_value_own = (key_value_sum + adapter_scale * key_value_extra).astype(jnp.bfloat16)
    pair_all = lax.all_gather(key_value_own, "tp", axis=1, tiled=True)
    key_width = pair_all.shape[1] // 2
    kv_heads = key_width // HEAD_DIM
    group = HEADS // kv_heads
    kv_index = tp_index * heads_here // group
    key_block = lax.dynamic_slice_in_dim(pair_all, kv_index * HEAD_DIM, HEAD_DIM, 1)
    value_block = lax.dynamic_slice_in_dim(pair_all, key_width + kv_index * HEAD_DIM, HEAD_DIM, 1)
    queries = rotate(query_plain.reshape(req_dev, slot_len, heads_here, HEAD_DIM)).astype(
        jnp.bfloat16
    )
    keys_one = rotate(key_block.astype(jnp.float32).reshape(req_dev, slot_len, 1, HEAD_DIM)).astype(
        jnp.bfloat16
    )[:, :, 0, :]
    values_one = value_block.reshape(req_dev, slot_len, HEAD_DIM)
    scale = 1.0 / math.sqrt(HEAD_DIM)
    scores = (
        jnp.einsum("rqhd,rkd->rhqk", queries, keys_one, preferred_element_type=jnp.float32) * scale
    )
    position = jnp.arange(slot_len, dtype=jnp.int32)
    allowed = (position[None, None, :] <= position[None, :, None]) & (
        position[None, None, :] < lengths[:, None, None]
    )
    scores = jnp.where(allowed[:, None, :, :], scores, -jnp.inf)
    highest = jnp.max(scores, axis=-1, keepdims=True)
    expo = jnp.exp(scores - highest)
    weights = (expo / jnp.sum(expo, axis=-1, keepdims=True)).astype(jnp.bfloat16)
    context = jnp.einsum("rhqk,rkd->rqhd", weights, values_one, preferred_element_type=jnp.float32)
    live_rows = position[None, :] < lengths[:, None]
    context = jnp.where(live_rows[:, :, None, None], context, 0.0)
    return context.reshape(rows_total, q_cols).astype(jnp.bfloat16)


def solution(mesh):
    return jax.shard_map(
        local,
        mesh=mesh,
        in_specs=(
            P("req", "tp"),
            P(None, "tp"),
            P(None, "tp"),
            P("req"),
            P("req"),
            P(),
            P("req", "tp", None),
            P("req", None, "tp"),
            P("req", None, "tp"),
        ),
        out_specs=P("req", "tp"),
        check_vma=False,
    )
```

profile of v0, /device:TPU:2, one launch (start us, length us, event | category | flops | bytes accessed | tf_op | source)
XLA Modules:
  0.0 358.5 jit_solution(2716103049818812552)
XLA Ops:
  6.5 0.0 copy-start
  6.5 0.0 all-gather.4.cloned.1.call-start
  6.5 0.7 all-gather.4.cloned.1.call-update
  7.3 0.0 all-gather.6.cloned.1.call-start
  7.3 0.7 all-gather.6.cloned.1.call-update
  8.0 0.0 all-gather.8.cloned.1.call-start
  8.1 0.7 all-gather.8.cloned.1.call-update
  9.4 1.3 fusion.39
  13.3 0.0 copy-start.4
  13.4 0.0 copy-start.6
  13.4 0.0 copy-start.2
  13.4 96.3 %all_gather.21 = bf16[128,16,128]{2,1,0:T(8,128)(2,1)} all-gather(bf16[1,16,128]{2,1,0:T(8,128)(2,1)} %param.17), channel_id=1, replica_groups=mesh['req'=128,'tp'=4] {'req'}, dimensions={0}, use_global_device_ids=true | all-gather | bytes 528384 | tf_op jit(solution)/shard_map/all_gather | solution.py:56
  109.7 0.0 copy-done.6
  109.7 0.1 fusion.9
  109.8 0.0 copy-done.4
  109.8 0.0 copy-done.2
  109.8 1.2 multiply_cosine_fusion
  111.0 0.0 all-gather.4.cloned.1.call-done
  111.0 0.0 copy-done
  111.0 2.4 fusion.45
  113.4 82.7 %all-gather.6.cloned.1.call-done = bf16[128,768,32]{1,2,0:T(8,128)(2,1)} async-done(((bf16[1,768,32]{1,2,0:T(8,128)(2,1)}), bf16[128,768,32]{1,2,0:T(8,128)(2,1)}) %all-gather.6.cloned.1.call-update) | async-done | bytes 6291472 | tf_op jit(solution)/shard_map/all_gather | solution.py:54
  196.1 0.8 dynamic-slice_select_fusion
  196.9 12.4 %all_gather.20 = bf16[1,3072,32]{1,2,0:T(8,128)(2,1)S(1)} all-gather(bf16[1,768,32]{1,2,0:T(8,128)(2,1)S(1)} %dynamic-slice_select_fusion), channel_id=1, replica_groups=mesh['req'=128,'tp'=4] {'tp'}, dimensions={1}, use_global_device_ids=true | all-gather | bytes 245760 | tf_op jit(solution)/shard_map/all_gather | solution.py:62
  209.3 2.0 fusion.6
  211.2 121.7 %all-gather.8.cloned.1.call-done = bf16[128,16,384]{2,1,0:T(8,128)(2,1)} async-done(((bf16[1,16,384]{2,1,0:T(8,128)(2,1)}), bf16[128,16,384]{2,1,0:T(8,128)(2,1)}) %all-gather.8.cloned.1.call-update) | async-done | bytes 1572880 | tf_op jit(solution)/shard_map/all_gather | solution.py:55
  332.9 1.0 fusion.2
  333.9 0.2 copy.21
  334.1 0.2 copy.30
  334.3 0.2 copy.31
  334.4 0.9 convolution_multiply_fusion.2
  335.3 0.0 copy-start.3
  335.3 0.0 copy-start.5
  335.4 0.0 copy-start.1
  335.4 2.2 fusion.5
  337.6 12.0 %all_gather.22 = bf16[256,512]{1,0:T(8,128)(2,1)S(1)} all-gather(bf16[256,128]{1,0:T(8,128)(2,1)S(1)} %fusion.5), channel_id=1, replica_groups=mesh['req'=128,'tp'=4] {'tp'}, dimensions={1}, use_global_device_ids=true | all-gather | bytes 327680 | tf_op jit(solution)/shard_map/all_gather | solution.py:82
  349.6 0.0 copy-done.3
  349.6 0.0 copy-done.5
  349.6 0.6 fusion.29
  350.2 0.0 copy-done.1
  350.2 0.0 copy-start.7
  350.2 0.1 fusion.10
  350.4 0.4 fusion.44
  350.7 0.1 fusion.7
  350.9 0.0 copy-done.7
  350.9 0.3 fusion.4
  351.2 0.8 copy.26
  (5 shorter events, 0.1 us)
Async XLA Ops:
  6.5 104.5 %copy-start = (bf16[3072,384]{1,0:T(8,128)(2,1)S(1)}, bf16[3072,384]{1,0:T(8,128)(2,1)}, u32[]{:S(2)}) copy-start(bf16[3072,384]{1,0:T(8,128)(2,1)} %param.10) | copy-start | bytes 7077892
  6.5 104.5 %all-gather.4.cloned.1.call-start = ((), (), s32[]{:S(2)}) async-start(), calls=%async_computation | async-start | bytes 1966080 | tf_op jit(solution)/shard_map/all_gather | solution.py:63
  7.3 188.8 %all-gather.6.cloned.1.call-start = ((), (), s32[]{:S(2)}) async-start(), calls=%async_computation.1 | async-start | bytes 6340608 | tf_op jit(solution)/shard_map/all_gather | solution.py:54
  8.0 324.9 %all-gather.8.cloned.1.call-start = ((), (), s32[]{:S(2)}) async-start(), calls=%async_computation.2 | async-start | bytes 1585152 | tf_op jit(solution)/shard_map/all_gather | solution.py:55
  13.3 96.5 %copy-start.4 = (f32[64]{0:T(128)}, f32[64]{0:T(128)S(1)}, u32[]{:S(2)}) copy-start(f32[64]{0:T(128)S(1)} %multiply_power_fusion) | copy-start | bytes 772
  13.4 96.3 %copy-start.6 = (pred[256]{0:T(512)(128)(4,1)}, pred[256]{0:T(512)(128)(4,1)S(1)}, u32[]{:S(2)}) copy-start(pred[256]{0:T(512)(128)(4,1)S(1)} %iota_compare_fusion.1) | copy-start | bytes 772
  13.4 96.4 %copy-start.2 = (f32[256]{0:T(256)}, f32[256]{0:T(256)S(1)}, u32[]{:S(2)}) copy-start(f32[256]{0:T(256)S(1)} %iota_convert_fusion) | copy-start | bytes 3076
  335.3 14.3 %copy-start.3 = (f32[256]{0:T(256)S(1)}, f32[256]{0:T(256)}, u32[]{:S(2)}) copy-start(f32[256]{0:T(256)} %copy-done.2) | copy-start | bytes 3076
  335.3 14.3 %copy-start.5 = (f32[64]{0:T(128)S(1)}, f32[64]{0:T(128)}, u32[]{:S(2)}) copy-start(f32[64]{0:T(128)} %copy-done.4) | copy-start | bytes 772
  335.4 14.9 %copy-start.1 = (f32[256,64]{1,0:T(8,128)S(1)}, f32[256,64]{1,0:T(8,128)}, u32[]{:S(2)}) copy-start(f32[256,64]{1,0:T(8,128)} %get-tuple-element.45) | copy-start | bytes 196612
  350.2 0.7 copy-start.7
Sparse Core Ops, SparseCore 0:
  9.5 37.5 all-gather.3
  50.2 145.7 all-gather.5
  199.1 133.7 all-gather.7
where the time goes:
time: 359 us
  waiting for transfers between devices  206 us (57%)
  blocking collectives  121 us (34%)
  between operations  16.5 us (5%)
  matrix products  9.02 us (3%)
  other arithmetic  4.29 us (1%)
    all_gather x1, waiting for transfers between devices, local(): lax.all_gather(query_up_store, 'req', axis=0, tiled=True)  122 us
    all_gather x1, blocking collectives, local(): lax.all_gather(key_value_store, 'req', axis=0, tiled=True)  96.3 us
    all_gather x1, waiting for transfers between devices, local(): lax.all_gather(down_store, 'req', axis=0, tiled=True)  82.7 us
    all_gather x1, blocking collectives, local(): full_down = lax.all_gather(adapter_down, 'tp', axis=1, tiled=True)  12.4 us
    all_gather x1, blocking collectives, local(): pair_all = lax.all_gather(key_value_own, 'tp', axis=1, tiled=True)  12 us
  transfers between devices with their start and end apart: 3, of which 2 were waited for; matrix products, arithmetic and copies ran while one was open for 2% of the time, Pallas kernels for 0%

commit v1 on v0

--- a/solution.py
+++ b/solution.py
@@ -8,6 +8,11 @@
 HEAD_DIM = 128
 adapter_scale = 0.5
 rope_base = 100000000000.0
+
+
+def gather_over(array, axis, dim):
+    outgoing = jnp.stack([array] * lax.axis_size(axis))
+    return jnp.concatenate(lax.all_to_all(outgoing, axis, 0, 0), axis=dim)
 
 
 def rotate(field):
@@ -52,7 +57,7 @@
     heads_here = q_cols // HEAD_DIM
     pooled = (
         lax.all_gather(down_store, "req", axis=0, tiled=True),
-        lax.all_gather(query_up_store, "req", axis=0, tiled=True),
+        gather_over(query_up_store, "req", 0),
         lax.all_gather(key_value_store, "req", axis=0, tiled=True),
     )
     own_slots = lookup_slots(adapter_ids, adapter_slot)

time: 359 us -> 242 us (0.67)
  waiting for transfers between devices: 206 us -> 16.2 us
  blocking collectives: 121 us -> 172 us
  starting transfers between devices: 0.08 us -> 20.6 us
    all_gather x1 -> x0, waiting for transfers between devices: 122 us -> none  [local(): lax.all_gather(query_up_store, 'req', axis=0, tiled=True)]
    all_gather x1, waiting for transfers between devices: 82.7 us -> 14.7 us  [local(): lax.all_gather(down_store, 'req', axis=0, tiled=True)]
    all_gather x1, blocking collectives: 96.3 us -> 148 us  [local(): lax.all_gather(key_value_store, 'req', axis=0, tiled=True)]
    all_to_all x0 -> x1, starting transfers between devices: none -> 20.6 us  [gather_over(): return jnp.concatenate(lax.all_to_all(outgoing, axis, 0, 0), axis=dim)]
  transfers between devices with their start and end apart: 3 -> 3, of which waited for: 2 -> 1; matrix products, arithmetic and copies ran while one was open for 2% -> 4% of each run, Pallas kernels for 0% -> 0%
where the time goes in v1:
time: 242 us
  blocking collectives  172 us (71%)
  starting transfers between devices  20.6 us (9%)
  between operations  17 us (7%)
  waiting for transfers between devices  16.2 us (7%)
  matrix products  9.05 us (4%)
  other arithmetic  3.64 us (2%)
  local copies, waits for them, and re-layouts  3.38 us (1%)
    all_gather x1, blocking collectives, local(): lax.all_gather(key_value_store, 'req', axis=0, tiled=True)  148 us
    all_to_all x1, starting transfers between devices, gather_over(): return jnp.concatenate(lax.all_to_all(outgoing, axis, 0, 0), axis=dim)  20.6 us
    all_gather x1, waiting for transfers between devices, local(): lax.all_gather(down_store, 'req', axis=0, tiled=True)  14.7 us
    all_gather x1, blocking collectives, local(): full_down = lax.all_gather(adapter_down, 'tp', axis=1, tiled=True)  12.1 us
    all_gather x1, blocking collectives, local(): pair_all = lax.all_gather(key_value_own, 'tp', axis=1, tiled=True)  11.8 us
  transfers between devices with their start and end apart: 3, of which 1 were waited for; matrix products, arithmetic and copies ran while one was open for 4% of the time, Pallas kernels for 0%

profile of v1, /device:TPU:2, one launch (start us, length us, event | category | flops | bytes accessed | tf_op | source)
XLA Modules:
  0.0 241.8 jit_solution(9095012345948005332)
XLA Ops:
  6.5 0.0 copy-start
  6.5 0.0 all-gather.3.cloned.1.call-start
  6.5 0.7 all-gather.3.cloned.1.call-update
  7.3 0.0 all-gather.5.cloned.1.call-start
  7.3 0.7 all-gather.5.cloned.1.call-update
  8.0 2.0 stack.2
  10.0 20.6 %all-to-all-start = ((bf16[128,1,16,384]{3,2,1,0:T(8,128)(2,1)}), bf16[128,1,16,384]{3,2,1,0:T(8,128)(2,1)}, u32[]{:S(2)}, u32[]{:S(2)}) async-start(bf16[128,1,16,384]{3,2,1,0:T(8,128)(2,1)} %stack.2), calls=%async_computation | async-start | bytes 3145728 | tf_op jit(solution)/shard_map/all_to_all | solution.py:15
  31.2 0.0 copy-done.9
  31.2 0.7 fusion.41
  34.7 0.0 copy-start.5
  34.7 0.0 copy-start.7
  34.7 0.0 copy-done.2
  34.7 0.0 copy-start.3
  34.7 148.1 %all_gather.18 = bf16[128,16,128]{2,1,0:T(8,128)(2,1)} all-gather(bf16[1,16,128]{2,1,0:T(8,128)(2,1)S(1)} %copy-done.2), channel_id=1, replica_groups=mesh['req'=128,'tp'=4] {'req'}, dimensions={0}, use_global_device_ids=true | all-gather | bytes 528384 | tf_op jit(solution)/shard_map/all_gather | solution.py:61
  182.9 0.1 fusion.9
  183.0 1.2 multiply_cosine_fusion
  184.2 0.0 copy-done.5
  184.2 0.0 copy-done.7
  184.2 0.0 copy-done.3
  184.2 0.0 all-gather.3.cloned.1.call-done
  184.2 0.0 copy-done
  184.2 2.4 fusion.47
  186.6 14.7 %all-gather.5.cloned.1.call-done = bf16[128,768,32]{1,2,0:T(8,128)(2,1)} async-done(((bf16[1,768,32]{1,2,0:T(8,128)(2,1)}), bf16[128,768,32]{1,2,0:T(8,128)(2,1)}) %all-gather.5.cloned.1.call-update) | async-done | bytes 6291472 | tf_op jit(solution)/shard_map/all_gather | solution.py:59
  201.4 0.8 dynamic-slice_select_fusion
  202.2 12.1 %all_gather.17 = bf16[1,3072,32]{1,2,0:T(8,128)(2,1)S(1)} all-gather(bf16[1,768,32]{1,2,0:T(8,128)(2,1)S(1)} %dynamic-slice_select_fusion), channel_id=1, replica_groups=mesh['req'=128,'tp'=4] {'tp'}, dimensions={1}, use_global_device_ids=true | all-gather | bytes 245760 | tf_op jit(solution)/shard_map/all_gather | solution.py:67
  214.2 2.0 fusion.6
  216.2 0.0 all-to-all-done
  216.2 1.0 fusion.2
  217.2 0.2 copy.21
  217.4 0.2 copy.30
  217.6 0.2 copy.31
  217.7 0.9 convolution_multiply_fusion.2
  218.6 0.0 copy-start.4
  218.6 0.0 copy-start.6
  218.7 0.0 copy-start.1
  218.7 2.2 fusion.5
  220.9 11.8 %all_gather.19 = bf16[256,512]{1,0:T(8,128)(2,1)S(1)} all-gather(bf16[256,128]{1,0:T(8,128)(2,1)S(1)} %fusion.5), channel_id=1, replica_groups=mesh['req'=128,'tp'=4] {'tp'}, dimensions={1}, use_global_device_ids=true | all-gather | bytes 327680 | tf_op jit(solution)/shard_map/all_gather | solution.py:87
  232.7 0.0 copy-done.4
  232.7 0.0 copy-done.6
  232.7 0.6 fusion.29
  233.3 0.0 copy-done.1
  233.3 0.0 copy-start.8
  233.3 0.1 fusion.10
  233.4 0.4 fusion.46
  233.8 0.1 fusion.7
  233.9 0.0 copy-done.8
  233.9 0.3 fusion.4
  234.2 0.8 copy.26
  (7 shorter events, 0.1 us)
Async XLA Ops:
  6.5 177.7 %copy-start = (bf16[3072,384]{1,0:T(8,128)(2,1)S(1)}, bf16[3072,384]{1,0:T(8,128)(2,1)}, u32[]{:S(2)}) copy-start(bf16[3072,384]{1,0:T(8,128)(2,1)} %param.10) | copy-start | bytes 7077892
  6.5 177.7 %all-gather.3.cloned.1.call-start = ((), (), s32[]{:S(2)}) async-start(), calls=%async_computation.1 | async-start | bytes 1966080 | tf_op jit(solution)/shard_map/all_gather | solution.py:68
  7.3 194.1 %all-gather.5.cloned.1.call-start = ((), (), s32[]{:S(2)}) async-start(), calls=%async_computation.2 | async-start | bytes 6340608 | tf_op jit(solution)/shard_map/all_gather | solution.py:59
  10.0 21.2 %copy-start.9 = (s32[64]{0:T(128)S(1)}, s32[64]{0:T(128)}, u32[]{:S(2)}) copy-start(s32[64]{0:T(128)} %param.14) | copy-start | bytes 772
  10.0 24.7 %copy-start.2 = (bf16[1,16,128]{2,1,0:T(8,128)(2,1)S(1)}, bf16[1,16,128]{2,1,0:T(8,128)(2,1)}, u32[]{:S(2)}) copy-start(bf16[1,16,128]{2,1,0:T(8,128)(2,1)} %param.17) | copy-start | bytes 12292
  10.0 206.2 %all-to-all-start = ((bf16[128,1,16,384]{3,2,1,0:T(8,128)(2,1)}), bf16[128,1,16,384]{3,2,1,0:T(8,128)(2,1)}, u32[]{:S(2)}, u32[]{:S(2)}) async-start(bf16[128,1,16,384]{3,2,1,0:T(8,128)(2,1)} %stack.2), calls=%async_computation | async-start | bytes 3145728 | tf_op jit(solution)/shard_map/all_to_all | solution.py:15
  34.7 149.5 %copy-start.5 = (f32[64]{0:T(128)}, f32[64]{0:T(128)S(1)}, u32[]{:S(2)}) copy-start(f32[64]{0:T(128)S(1)} %multiply_power_fusion) | copy-start | bytes 772
  34.7 149.5 %copy-start.7 = (pred[256]{0:T(512)(128)(4,1)}, pred[256]{0:T(512)(128)(4,1)S(1)}, u32[]{:S(2)}) copy-start(pred[256]{0:T(512)(128)(4,1)S(1)} %iota_compare_fusion.1) | copy-start | bytes 772
  34.7 149.5 %copy-start.3 = (f32[256]{0:T(256)}, f32[256]{0:T(256)S(1)}, u32[]{:S(2)}) copy-start(f32[256]{0:T(256)S(1)} %iota_convert_fusion) | copy-start | bytes 3076
  218.6 14.0 %copy-start.4 = (f32[256]{0:T(256)S(1)}, f32[256]{0:T(256)}, u32[]{:S(2)}) copy-start(f32[256]{0:T(256)} %copy-done.3) | copy-start | bytes 3076
  218.6 14.0 %copy-start.6 = (f32[64]{0:T(128)S(1)}, f32[64]{0:T(128)}, u32[]{:S(2)}) copy-start(f32[64]{0:T(128)} %copy-done.5) | copy-start | bytes 772
  218.7 14.6 %copy-start.1 = (f32[256,64]{1,0:T(8,128)S(1)}, f32[256,64]{1,0:T(8,128)}, u32[]{:S(2)}) copy-start(f32[256,64]{1,0:T(8,128)} %get-tuple-element.45) | copy-start | bytes 196612
  233.3 0.6 copy-start.8
Sparse Core Ops, SparseCore 0:
  9.5 37.5 all-gather.2
  50.2 151.0 all-gather.4
